TPU v7x, 512 devices: a whole 4x8x8 slice. The times are simulated.
512 devices in a mesh: dp: 8 (over y_hi, x), expert: 64 (over y_lo, z, core).
Axes of the slice: x: 4, y: 8 (y_hi: 2, y_lo: 4; y = y_hi * 4 + y_lo), z: 8, core: 2. Of those that a mesh axis runs over, the one named last changes fastest.
Arguments:
- tokens: bfloat16 [8192, 2560], P(('dp', 'expert')), may hold values from -6 to 6
- grad_out: bfloat16 [8192, 2560], P(('dp', 'expert')), may hold values from -6 to 6
- expert_ids: int32 [8192, 2], P(('dp', 'expert')), may hold values from 0 to 63, as said below
- gates: bfloat16 [8192, 2], P(('dp', 'expert')), may hold values from 0.099609375 to 1
- w_gate: bfloat16 [64, 2560, 1024], P('expert', None, 'dp'), may hold values from -0.125 to 0.125
- w_up: bfloat16 [64, 2560, 1024], P('expert', None, 'dp'), may hold values from -0.125 to 0.125
- w_down: bfloat16 [64, 1024, 2560], P('expert', 'dp'), may hold values from -0.1875 to 0.1875
Outputs:
- out_tokens: bfloat16 [8192, 2560], P(('dp', 'expert'))
- grad_tokens: bfloat16 [8192, 2560], P(('dp', 'expert'))
- grad_gate: bfloat16 [64, 2560, 1024], P('expert', None, 'dp')
- grad_up: bfloat16 [64, 2560, 1024], P('expert', None, 'dp')
- grad_down: bfloat16 [64, 1024, 2560], P('expert', 'dp')
Inputs may be any that keep to these rules, and one draw needn't show every extreme that they name: `expert_ids`: each token names 2 different experts. Over the tokens of all devices at one index of expert taken together, one expert, the same at every index, is named exactly 8 times; a second one, also the same at every index, exactly 5 times; every other expert at most 5 times.
All inputs are finite; a program needn't handle non-finite values.
Results may differ from a plain program's by a relative error of at most 0.019.
Values may be sent and summed in bfloat16 or wider, within the bound.
No kernel may reach another device: no remote copies, remote signals or barrier semaphores. Data moves between devices by JAX's collectives and lax.ppermute only.
A program may use at most 128 MiB of HBM per device.

v0:
```python
import jax
import jax.numpy as jnp
from jax import lax
from jax.sharding import PartitionSpec as P


def expert_rows(rows_in, cot_in, gate_weight, up_weight, down_weight):
    gate_pre = jnp.dot(rows_in, gate_weight, preferred_element_type=jnp.float32)
    up_pre = jnp.dot(rows_in, up_weight, preferred_element_type=jnp.float32)
    hidden = (jax.nn.silu(gate_pre) * up_pre).astype(jnp.bfloat16)
    partial_value = jnp.dot(hidden, down_weight, preferred_element_type=jnp.float32).astype(
        jnp.bfloat16
    )
    first_dim = (((0,), (0,)), ((), ()))
    last_dim = (((1,), (1,)), ((), ()))
    grad_down = lax.dot_general(hidden, cot_in, first_dim, preferred_element_type=jnp.float32)
    d_hidden = lax.dot_general(cot_in, down_weight, last_dim, preferred_element_type=jnp.float32)
    sig = jax.nn.sigmoid(gate_pre)
    d_gate = (d_hidden * up_pre * sig * (1.0 + gate_pre * (1.0 - sig))).astype(jnp.bfloat16)
    d_up = (d_hidden * gate_pre * sig).astype(jnp.bfloat16)
    grad_gate = lax.dot_general(rows_in, d_gate, first_dim, preferred_element_type=jnp.float32)
    grad_up = lax.dot_general(rows_in, d_up, first_dim, preferred_element_type=jnp.float32)
    back_term = lax.dot_general(d_gate, gate_weight, last_dim, preferred_element_type=jnp.float32)
    back_term = (
        back_term + lax.dot_general(d_up, up_weight, last_dim, preferred_element_type=jnp.float32)
    ).astype(jnp.bfloat16)
    return (partial_value, back_term, grad_gate, grad_up, grad_down)


def fill_slots(slot_index, slot_total, assigned, top_count, group_tokens, cot_rows):
    owner = jnp.full((slot_total,), assigned, jnp.int32)
    owner = owner.at[slot_index].set(jnp.arange(assigned, dtype=jnp.int32), mode="drop")
    filled = owner < assigned
    safe = jnp.where(filled, owner, 0)
    token_rows = jnp.take(group_tokens, safe // top_count, axis=0)
    cot_taken = jnp.take(cot_rows, safe, axis=0)
    token_rows = jnp.where(filled[:, None], token_rows, jnp.zeros((), token_rows.dtype))
    cot_taken = jnp.where(filled[:, None], cot_taken, jnp.zeros((), cot_taken.dtype))
    return (token_rows, cot_taken)


def collect_slots(values, slot_index, weights):
    taken = jnp.take(values, slot_index.reshape(-1), axis=0, mode="fill", fill_value=0)
    taken = taken.reshape(slot_index.shape[0], slot_index.shape[1], values.shape[1]).astype(
        jnp.float32
    )
    if weights is None:
        return jnp.sum(taken, axis=1)
    return jnp.sum(weights.astype(jnp.float32)[:, :, None] * taken, axis=1)


def body(tokens, grad_out, expert_ids, gates, w_gate, w_up, w_down):
    dp_count = lax.axis_size("dp")
    experts = lax.axis_size("expert")
    local_rows = tokens.shape[0]
    feature_width = tokens.shape[1]
    top_count = expert_ids.shape[1]
    group_rows = dp_count * local_rows
    assigned = group_rows * top_count
    mean_slots = assigned // experts
    cap_hot = 2 * mean_slots
    group_tokens, group_grads, group_ids, group_gates = (
        lax.all_gather(tokens, "dp", axis=0, tiled=True),
        lax.all_gather(grad_out, "dp", axis=0, tiled=True),
        lax.all_gather(expert_ids, "dp", axis=0, tiled=True),
        lax.all_gather(gates, "dp", axis=0, tiled=True),
    )
    flat_ids = group_ids.reshape(-1)
    expert_range = jnp.arange(experts, dtype=jnp.int32)
    member = (flat_ids[:, None] == expert_range[None, :]).astype(jnp.int32)
    before = jnp.sum((jnp.cumsum(member, axis=0) - member) * member, axis=1)
    cot_rows = (
        (group_gates.astype(jnp.float32)[:, :, None] * group_grads.astype(jnp.float32)[:, None, :])
        .astype(jnp.bfloat16)
        .reshape(assigned, feature_width)
    )
    goes_out = jnp.ones(flat_ids.shape, dtype=bool)
    slot_count = experts * cap_hot
    slot_of = jnp.where(goes_out, flat_ids * cap_hot + before, slot_count).astype(jnp.int32)
    send_rows, send_cot = fill_slots(
        slot_of, slot_count, assigned, top_count, group_tokens, cot_rows
    )
    arrived_rows, arrived_cot = (
        lax.all_to_all(
            send_rows.reshape(experts, cap_hot, feature_width),
            "expert",
            split_axis=0,
            concat_axis=0,
            tiled=True,
        ),
        lax.all_to_all(
            send_cot.reshape(experts, cap_hot, feature_width),
            "expert",
            split_axis=0,
            concat_axis=0,
            tiled=True,
        ),
    )
    partial_value, back_term, grad_gate, grad_up, grad_down = expert_rows(
        arrived_rows.reshape(slot_count, feature_width),
        arrived_cot.reshape(slot_count, feature_width),
        w_gate[0],
        w_up[0],
        w_down[0],
    )
    return_partial, return_back = (
        lax.all_to_all(
            partial_value.reshape(experts, cap_hot, feature_width),
            "expert",
            split_axis=0,
            concat_axis=0,
            tiled=True,
        ),
        lax.all_to_all(
            back_term.reshape(experts, cap_hot, feature_width),
            "expert",
            split_axis=0,
            concat_axis=0,
            tiled=True,
        ),
    )
    slot_pairs = slot_of.reshape(group_rows, top_count)
    out_part = collect_slots(
        return_partial.reshape(slot_count, feature_width), slot_pairs, group_gates
    )
    back_part = collect_slots(return_back.reshape(slot_count, feature_width), slot_pairs, None)
    out_sum, back_sum = (
        lax.psum_scatter(
            out_part.astype(jnp.bfloat16), "dp", scatter_dimension=0, tiled=True
        ).astype(jnp.float32),
        lax.psum_scatter(
            back_part.astype(jnp.bfloat16), "dp", scatter_dimension=0, tiled=True
        ).astype(jnp.float32),
    )
    return (
        out_sum.astype(jnp.bfloat16),
        back_sum.astype(jnp.bfloat16),
        grad_gate.astype(jnp.bfloat16)[None],
        grad_up.astype(jnp.bfloat16)[None],
        grad_down.astype(jnp.bfloat16)[None],
    )


def solution(mesh):
    in_specs = (
        P(("dp", "expert"), None),
        P(("dp", "expert"), None),
        P(("dp", "expert"), None),
        P(("dp", "expert"), None),
        P("expert", None, "dp"),
        P("expert", None, "dp"),
        P("expert", "dp", None),
    )
    out_specs = (
        P(("dp", "expert"), None),
        P(("dp", "expert"), None),
        P("expert", None, "dp"),
        P("expert", None, "dp"),
        P("expert", "dp", None),
    )
    return jax.shard_map(body, mesh=mesh, in_specs=in_specs, out_specs=out_specs, check_vma=False)
```

profile of v0, /device:TPU:2, one launch (start us, length us, event | category | flops | bytes accessed | tf_op | source)
XLA Modules:
  0.0 699.0 jit_solution(2245142333885996936)
XLA Ops:
  7.2 0.0 copy-start
  7.2 29.1 %all-gather.1 = s32[8,16,2]{1,2,0:T(2,128)S(1)} all-gather(s32[1,16,2]{1,2,0:T(2,128)} %bitcast.86), channel_id=1, replica_groups=mesh['dp'=8,'expert'=64] {'dp'}, dimensions={0}, use_global_device_ids=true | all-gather | bytes 1152 | tf_op jit(solution)/shard_map/all_gather | solution.py:65
  36.3 0.1 copy.28
  36.5 0.1 eq.25
  36.6 0.1 eq.29
  36.7 0.1 copy.32
  36.9 0.1 mul.77
  37.0 0.6 reduce-window.6
  37.6 0.2 slice_reduce_fusion
  37.9 0.1 fusion.25
  38.0 1.4 scatter_custom_fusion
  39.4 25.7 %all-gather = bf16[8,16,2]{1,2,0:T(2,128)(2,1)S(1)} all-gather(bf16[1,16,2]{1,2,0:T(2,128)(2,1)} %bitcast.88), channel_id=1, replica_groups=mesh['dp'=8,'expert'=64] {'dp'}, dimensions={0}, use_global_device_ids=true | all-gather | bytes 576 | tf_op jit(solution)/shard_map/all_gather | solution.py:66
  65.2 0.1 copy.34
  65.3 0.1 mul.84
  65.5 0.1 broadcast_in_dim.82
  65.6 0.1 broadcast_in_dim.87
  65.7 0.3 copy-done.3
  65.9 0.1 broadcast_in_dim.79
  66.0 40.3 %all_gather.14 = bf16[128,2560]{1,0:T(8,128)(2,1)S(1)} all-gather(bf16[16,2560]{1,0:T(8,128)(2,1)} %param.9), channel_id=1, replica_groups=mesh['dp'=8,'expert'=64] {'dp'}, dimensions={0}, use_global_device_ids=true | all-gather | bytes 737280 | tf_op jit(solution)/shard_map/all_gather | solution.py:63
  106.4 46.3 %all_gather.15 = bf16[128,2560]{1,0:T(8,128)(2,1)S(1)} all-gather(bf16[16,2560]{1,0:T(8,128)(2,1)} %param.10), channel_id=1, replica_groups=mesh['dp'=8,'expert'=64] {'dp'}, dimensions={0}, use_global_device_ids=true | all-gather | bytes 737280 | tf_op jit(solution)/shard_map/all_gather | solution.py:64
  152.7 2.2 mul.86
  154.9 4.5 mul.87
  159.4 3.5 gather_fusion
  162.9 1.9 multiply_convert_fusion
  164.9 3.5 gather_fusion.1
  168.4 4.0 fusion.8
  172.3 73.2 %all_to_all.20 = bf16[64,8,2560]{2,1,0:T(8,128)(2,1)S(1)} all-to-all(bf16[64,8,2560]{2,1,0:T(8,128)(2,1)S(1)} %get-tuple-element.14), channel_id=1, replica_groups=mesh['dp'=8,'expert'=64] {'expert'}, dimensions={0} | all-to-all | bytes 5242880 | tf_op jit(solution)/shard_map/all_to_all | solution.py:84
  245.5 12.7 %all-to-all-start.2 = ((bf16[64,8,2560]{2,1,0:T(8,128)(2,1)}), bf16[64,8,2560]{2,1,0:T(8,128)(2,1)}, u32[]{:S(2)}, u32[]{:S(2)}) async-start(bf16[64,8,2560]{2,1,0:T(8,128)(2,1)} %get-tuple-element.13), calls=%async_computation.3 | async-start | bytes 5242880 | tf_op jit(solution)/shard_map/all_to_all | solution.py:91
  258.2 0.0 copy-start.2
  258.2 2.0 fusion.11
  260.2 0.0 copy-done.2
  260.2 1.5 fusion.13
  261.8 58.2 %all-to-all-done.2 = bf16[64,8,2560]{2,1,0:T(8,128)(2,1)} async-done(((bf16[64,8,2560]{2,1,0:T(8,128)(2,1)}), bf16[64,8,2560]{2,1,0:T(8,128)(2,1)}, u32[]{:S(2)}, u32[]{:S(2)}) %all-to-all-start.2) | async-done | bytes 2621472 | tf_op jit(solution)/shard_map/all_to_all | solution.py:91
  319.9 0.0 copy-done
  319.9 3.3 multiply_convert_fusion.1
  323.2 0.6 copy-done.7
  323.9 2.3 fusion.1
  326.2 16.2 %all-to-all-start.1 = ((bf16[64,8,2560]{2,1,0:T(8,128)(2,1)}), bf16[64,8,2560]{2,1,0:T(8,128)(2,1)}, u32[]{:S(2)}, u32[]{:S(2)}) async-start(bf16[64,8,2560]{2,1,0:T(8,128)(2,1)} %fusion.1), calls=%async_computation.1 | async-start | bytes 5242880 | tf_op jit(solution)/shard_map/all_to_all | solution.py:107
  342.4 0.0 copy-start.1
  342.4 0.0 copy-start.5
  342.4 2.1 fusion.20
  344.5 0.0 copy-done.1
  344.5 0.0 copy-done.5
  344.5 2.4 fusion
  347.0 57.2 %all-to-all-done.1 = bf16[64,8,2560]{2,1,0:T(8,128)(2,1)} async-done(((bf16[64,8,2560]{2,1,0:T(8,128)(2,1)}), bf16[64,8,2560]{2,1,0:T(8,128)(2,1)}, u32[]{:S(2)}, u32[]{:S(2)}) %all-to-all-start.1) | async-done | bytes 2621472 | tf_op jit(solution)/shard_map/all_to_all | solution.py:107
  404.2 16.2 %all-to-all-start.3 = ((bf16[64,8,2560]{2,1,0:T(8,128)(2,1)}), bf16[64,8,2560]{2,1,0:T(8,128)(2,1)}, u32[]{:S(2)}, u32[]{:S(2)}) async-start(bf16[64,8,2560]{2,1,0:T(8,128)(2,1)} %fusion), calls=%async_computation.4 | async-start | bytes 5242880 | tf_op jit(solution)/shard_map/all_to_all | solution.py:114
  420.4 0.0 reduce-scatter.5.cloned.1.call-start
  420.4 5.9 gather_fusion.2
  426.3 55.8 %all-to-all-done.3 = bf16[64,8,2560]{2,1,0:T(8,128)(2,1)} async-done(((bf16[64,8,2560]{2,1,0:T(8,128)(2,1)}), bf16[64,8,2560]{2,1,0:T(8,128)(2,1)}, u32[]{:S(2)}, u32[]{:S(2)}) %all-to-all-start.3) | async-done | bytes 2621472 | tf_op jit(solution)/shard_map/all_to_all | solution.py:114
  482.1 6.0 gather_fusion.3
  488.1 4.0 broadcast_select_fusion
  492.1 4.0 reshape.131
  496.1 5.4 reduce_sum.35
  501.4 0.0 reduce-scatter.5.cloned.1.call-update
  501.5 0.3 reduce-scatter.3.cloned.1.call-start
  501.7 0.0 copy-start.4
  501.8 4.4 reshape.132
  506.2 6.3 multiply_reduce_fusion
  512.5 0.0 reduce-scatter.3.cloned.1.call-update
  512.5 3.2 fusion.4
  515.7 1.7 fusion.3
  517.4 1.7 fusion.2
  519.2 80.9 %reduce-scatter.5.cloned.1.call-done = bf16[16,2560]{1,0:T(8,128)(2,1)} async-done(((bf16[128,2560]{1,0:T(8,128)(2,1)}), bf16[16,2560]{1,0:T(8,128)(2,1)}) %reduce-scatter.5.cloned.1.call-update) | async-done | bytes 81936 | tf_op jit(solution)/shard_map/reduce_scatter | solution.py:131
  600.1 92.1 %reduce-scatter.3.cloned.1.call-done = bf16[16,2560]{1,0:T(8,128)(2,1)} async-done(((bf16[128,2560]{1,0:T(8,128)(2,1)}), bf16[16,2560]{1,0:T(8,128)(2,1)}) %reduce-scatter.3.cloned.1.call-update) | async-done | bytes 81936 | tf_op jit(solution)/shard_map/reduce_scatter | solution.py:128
  (18 shorter events, 0.1 us)
Async XLA Ops:
  7.2 312.8 %copy-start = (bf16[1,128,2560]{2,1,0:T(8,128)(2,1)S(1)}, bf16[1,128,2560]{2,1,0:T(8,128)(2,1)}, u32[]{:S(2)}) copy-start(bf16[1,128,2560]{2,1,0:T(8,128)(2,1)} %param.15) | copy-start | bytes 1966084
  65.3 0.6 copy-start.3
  245.5 74.4 %all-to-all-start.2 = ((bf16[64,8,2560]{2,1,0:T(8,128)(2,1)}), bf16[64,8,2560]{2,1,0:T(8,128)(2,1)}, u32[]{:S(2)}, u32[]{:S(2)}) async-start(bf16[64,8,2560]{2,1,0:T(8,128)(2,1)} %get-tuple-element.13), calls=%async_computation.3 | async-start | bytes 5242880 | tf_op jit(solution)/shard_map/all_to_all | solution.py:91
  258.2 2.0 copy-start.2
  323.2 0.6 copy-start.7
  326.2 77.9 %all-to-all-start.1 = ((bf16[64,8,2560]{2,1,0:T(8,128)(2,1)}), bf16[64,8,2560]{2,1,0:T(8,128)(2,1)}, u32[]{:S(2)}, u32[]{:S(2)}) async-start(bf16[64,8,2560]{2,1,0:T(8,128)(2,1)} %fusion.1), calls=%async_computation.1 | async-start | bytes 5242880 | tf_op jit(solution)/shard_map/all_to_all | solution.py:107
  342.4 2.1 copy-start.1
  342.4 2.1 copy-start.5
  404.2 77.9 %all-to-all-start.3 = ((bf16[64,8,2560]{2,1,0:T(8,128)(2,1)}), bf16[64,8,2560]{2,1,0:T(8,128)(2,1)}, u32[]{:S(2)}, u32[]{:S(2)}) async-start(bf16[64,8,2560]{2,1,0:T(8,128)(2,1)} %fusion), calls=%async_computation.4 | async-start | bytes 5242880 | tf_op jit(solution)/shard_map/all_to_all | solution.py:114
  420.4 179.7 %reduce-scatter.5.cloned.1.call-start = ((), (), s32[]{:S(2)}) async-start(), calls=%async_computation.7 | async-start | bytes 737280 | tf_op jit(solution)/shard_map/reduce_scatter | solution.py:131
  501.5 190.7 %reduce-scatter.3.cloned.1.call-start = ((), (), s32[]{:S(2)}) async-start(), calls=%async_computation.6 | async-start | bytes 737280 | tf_op jit(solution)/shard_map/reduce_scatter | solution.py:128
  501.7 4.4 copy-start.4
  515.7 1.7 copy-start.6
Sparse Core Ops, SparseCore 0:
  501.6 98.4 reduce-scatter.4
  605.1 86.9 reduce-scatter.2
where the time goes:
time: 700 us; the launch traced here: 699 us
  waiting for transfers between devices  344 us (49%)
  blocking collectives  215 us (31%)
  starting transfers between devices  45.4 us (6%)
  local copies, waits for them, and re-layouts  37.7 us (5%)
  other arithmetic  22.5 us (3%)
  matrix products  20.3 us (3%)
  between operations  14.3 us (2%)
    reduce_scatter x1, waiting for transfers between devices, body(): lax.psum_scatter(out_part.astype(jnp.bfloat16), 'dp', scatter_dimension=0...  92.1 us
    reduce_scatter x1, waiting for transfers between devices, body(): lax.psum_scatter(back_part.astype(jnp.bfloat16), 'dp', scatter_dimension=...  80.9 us
    all_to_all x1, blocking collectives, body(): lax.all_to_all(send_rows.reshape(experts, cap_hot, feature_width), 'exper...  73.2 us
    all_to_all x1, waiting for transfers between devices, body(): lax.all_to_all(send_cot.reshape(experts, cap_hot, feature_width), 'expert...  58.2 us
    all_to_all x1, waiting for transfers between devices, body(): lax.all_to_all(partial_value.reshape(experts, cap_hot, feature_width), 'e...  57.2 us
    all_to_all x1, waiting for transfers between devices, body(): lax.all_to_all(back_term.reshape(experts, cap_hot, feature_width), 'exper...  55.8 us
    all_gather x1, blocking collectives, body(): lax.all_gather(grad_out, 'dp', axis=0, tiled=True)  46.3 us
    all_gather x1, blocking collectives, body(): lax.all_gather(tokens, 'dp', axis=0, tiled=True)  40.3 us
  transfers between devices with their start and end apart: 5, of which 5 were waited for; matrix products, arithmetic and copies ran while one was open for 4% of the time, Pallas kernels for 0%

commit v1 on v0

--- a/solution.py
+++ b/solution.py
@@ -61,7 +61,9 @@
     cap_hot = 2 * mean_slots
     group_tokens, group_grads, group_ids, group_gates = (
         lax.all_gather(tokens, "dp", axis=0, tiled=True),
-        lax.all_gather(grad_out, "dp", axis=0, tiled=True),
+        jnp.concatenate(
+            lax.all_to_all(jnp.stack([grad_out] * lax.axis_size("dp")), "dp", 0, 0), axis=0
+        ),
         lax.all_gather(expert_ids, "dp", axis=0, tiled=True),
         lax.all_gather(gates, "dp", axis=0, tiled=True),
     )

time: 700 us -> 671 us (0.959)
  blocking collectives: 215 us -> 172 us
  starting transfers between devices: 45.4 us -> 56.3 us
  waiting for transfers between devices: 344 us -> 351 us
    all_gather x1 -> x0, blocking collectives: 46.3 us -> none  [body(): lax.all_gather(grad_out, 'dp', axis=0, tiled=True)]
    reduce_scatter x1, waiting for transfers between devices: 80.9 us -> 92.1 us  [body(): lax.psum_scatter(back_part.astype(jnp.bfloat16), 'dp', scatter_dimension=...]
    all_to_all x0 -> x1, starting transfers between devices: none -> 10.1 us  [body(): lax.all_to_all(jnp.stack([grad_out] * lax.axis_size('dp')), 'dp', 0, 0)]
  transfers between devices with their start and end apart: 5 -> 6, of which waited for: 5 -> 5; matrix products, arithmetic and copies ran while one was open for 4% -> 5% of each run, Pallas kernels for 0% -> 0%
where the time goes in v1:
time: 671 us; the launch traced here: 670 us
  waiting for transfers between devices  351 us (52%)
  blocking collectives  172 us (26%)
  starting transfers between devices  56.3 us (8%)
  local copies, waits for them, and re-layouts  36.4 us (5%)
  other arithmetic  22.5 us (3%)
  matrix products  19 us (3%)
  between operations  14.3 us (2%)
    reduce_scatter x1, waiting for transfers between devices, body(): lax.psum_scatter(back_part.astype(jnp.bfloat16), 'dp', scatter_dimension=...  92.1 us
    reduce_scatter x1, waiting for transfers between devices, body(): lax.psum_scatter(out_part.astype(jnp.bfloat16), 'dp', scatter_dimension=0...  85.3 us
    all_to_all x1, blocking collectives, body(): lax.all_to_all(send_rows.reshape(experts, cap_hot, feature_width), 'exper...  75.1 us
    all_to_all x1, waiting for transfers between devices, body(): lax.all_to_all(back_term.reshape(experts, cap_hot, feature_width), 'exper...  59.4 us
    all_to_all x1, waiting for transfers between devices, body(): lax.all_to_all(send_cot.reshape(experts, cap_hot, feature_width), 'expert...  58.2 us
    all_to_all x1, waiting for transfers between devices, body(): lax.all_to_all(partial_value.reshape(experts, cap_hot, feature_width), 'e...  55.6 us
    all_gather x1, blocking collectives, body(): lax.all_gather(tokens, 'dp', axis=0, tiled=True)  40.1 us
    all_gather x1, blocking collectives, body(): lax.all_gather(expert_ids, 'dp', axis=0, tiled=True)  33.6 us
  transfers between devices with their start and end apart: 6, of which 5 were waited for; matrix products, arithmetic and copies ran while one was open for 5% of the time, Pallas kernels for 0%

profile of v1, /device:TPU:2, one launch (start us, length us, event | category | flops | bytes accessed | tf_op | source)
XLA Modules:
  0.0 670.4 jit_solution(1115932848486051379)
XLA Ops:
  7.2 0.0 copy-start
  7.2 0.0 copy-start.12
  7.2 1.8 stack.2
  9.0 10.1 %all-to-all-start.2 = ((bf16[8,16,2560]{2,1,0:T(8,128)(2,1)}), bf16[8,16,2560]{2,1,0:T(8,128)(2,1)S(1)}, u32[]{:S(2)}, u32[]{:S(2)}) async-start(bf16[8,16,2560]{2,1,0:T(8,128)(2,1)} %stack.2), calls=%async_computation.3 | async-start | bytes 1310720 | tf_op jit(solution)/shard_map/all_to_all | solution.py:65
  19.1 33.6 %all-gather.1 = s32[8,16,2]{1,2,0:T(2,128)S(1)} all-gather(s32[1,16,2]{1,2,0:T(2,128)} %bitcast.88), channel_id=1, replica_groups=mesh['dp'=8,'expert'=64] {'dp'}, dimensions={0}, use_global_device_ids=true | all-gather | bytes 1152 | tf_op jit(solution)/shard_map/all_gather | solution.py:67
  52.8 0.1 copy.28
  52.9 0.1 eq.29
  53.0 0.1 eq.25
  53.2 0.6 reduce-window.6
  53.8 0.2 slice_reduce_fusion
  54.0 0.1 copy.32
  54.2 0.1 mul.77
  54.3 0.1 fusion.25
  54.4 1.4 scatter_custom_fusion
  55.9 0.1 broadcast_in_dim.79
  56.0 0.1 broadcast_in_dim.82
  56.1 0.1 broadcast_in_dim.87
  56.2 0.0 copy-done.12
  56.2 22.7 %all-gather = bf16[8,16,2]{1,2,0:T(2,128)(2,1)S(1)} all-gather(bf16[1,16,2]{1,2,0:T(2,128)(2,1)S(1)} %bitcast.90), channel_id=1, replica_groups=mesh['dp'=8,'expert'=64] {'dp'}, dimensions={0}, use_global_device_ids=true | all-gather | bytes 576 | tf_op jit(solution)/shard_map/all_gather | solution.py:68
  78.8 0.1 copy.34
  79.0 0.1 mul.84
  79.1 0.5 copy-done.4
  79.6 40.1 %all_gather.11 = bf16[128,2560]{1,0:T(8,128)(2,1)S(1)} all-gather(bf16[16,2560]{1,0:T(8,128)(2,1)S(1)} %copy-done.11), channel_id=1, replica_groups=mesh['dp'=8,'expert'=64] {'dp'}, dimensions={0}, use_global_device_ids=true | all-gather | bytes 737280 | tf_op jit(solution)/shard_map/all_gather | solution.py:63
  119.7 3.5 gather_fusion
  123.2 0.0 all-to-all-done.2
  123.2 0.2 bitcast_convert_fusion
  123.4 0.9 mul.86
  124.3 2.9 mul.87
  127.2 1.9 multiply_convert_fusion
  129.1 3.5 gather_fusion.1
  132.6 3.9 fusion.8
  136.5 75.1 %all_to_all.25 = bf16[64,8,2560]{2,1,0:T(8,128)(2,1)S(1)} all-to-all(bf16[64,8,2560]{2,1,0:T(8,128)(2,1)S(1)} %get-tuple-element.14), channel_id=1, replica_groups=mesh['dp'=8,'expert'=64] {'expert'}, dimensions={0} | all-to-all | bytes 5242880 | tf_op jit(solution)/shard_map/all_to_all | solution.py:86
  211.7 12.9 %all-to-all-start.3 = ((bf16[64,8,2560]{2,1,0:T(8,128)(2,1)}), bf16[64,8,2560]{2,1,0:T(8,128)(2,1)}, u32[]{:S(2)}, u32[]{:S(2)}) async-start(bf16[64,8,2560]{2,1,0:T(8,128)(2,1)} %get-tuple-element.13), calls=%async_computation.4 | async-start | bytes 5242880 | tf_op jit(solution)/shard_map/all_to_all | solution.py:93
  224.5 0.0 copy-start.2
  224.5 2.0 fusion.11
  226.5 1.5 fusion.13
  228.1 58.2 %all-to-all-done.3 = bf16[64,8,2560]{2,1,0:T(8,128)(2,1)} async-done(((bf16[64,8,2560]{2,1,0:T(8,128)(2,1)}), bf16[64,8,2560]{2,1,0:T(8,128)(2,1)}, u32[]{:S(2)}, u32[]{:S(2)}) %all-to-all-start.3) | async-done | bytes 2621472 | tf_op jit(solution)/shard_map/all_to_all | solution.py:93
  286.3 3.3 multiply_convert_fusion.1
  289.6 0.0 copy-done.3
  289.6 0.8 fusion.20
  290.5 0.3 copy-done.1
  290.8 2.4 fusion
  293.1 16.5 %all-to-all-start.4 = ((bf16[64,8,2560]{2,1,0:T(8,128)(2,1)}), bf16[64,8,2560]{2,1,0:T(8,128)(2,1)}, u32[]{:S(2)}, u32[]{:S(2)}) async-start(bf16[64,8,2560]{2,1,0:T(8,128)(2,1)} %fusion), calls=%async_computation.5 | async-start | bytes 5242880 | tf_op jit(solution)/shard_map/all_to_all | solution.py:116
  309.7 2.4 fusion.1
  312.1 59.4 %all-to-all-done.4 = bf16[64,8,2560]{2,1,0:T(8,128)(2,1)} async-done(((bf16[64,8,2560]{2,1,0:T(8,128)(2,1)}), bf16[64,8,2560]{2,1,0:T(8,128)(2,1)}, u32[]{:S(2)}, u32[]{:S(2)}) %all-to-all-start.4) | async-done | bytes 2621472 | tf_op jit(solution)/shard_map/all_to_all | solution.py:116
  371.4 16.2 %all-to-all-start.1 = ((bf16[64,8,2560]{2,1,0:T(8,128)(2,1)}), bf16[64,8,2560]{2,1,0:T(8,128)(2,1)}, u32[]{:S(2)}, u32[]{:S(2)}) async-start(bf16[64,8,2560]{2,1,0:T(8,128)(2,1)} %fusion.1), calls=%async_computation.1 | async-start | bytes 5242880 | tf_op jit(solution)/shard_map/all_to_all | solution.py:109
  387.6 0.3 reduce-scatter.3.cloned.1.call-start
  387.9 5.9 gather_fusion.3
  393.8 55.6 %all-to-all-done.1 = bf16[64,8,2560]{2,1,0:T(8,128)(2,1)} async-done(((bf16[64,8,2560]{2,1,0:T(8,128)(2,1)}), bf16[64,8,2560]{2,1,0:T(8,128)(2,1)}, u32[]{:S(2)}, u32[]{:S(2)}) %all-to-all-start.1) | async-done | bytes 2621472 | tf_op jit(solution)/shard_map/all_to_all | solution.py:109
  449.3 5.9 gather_fusion.2
  455.3 3.9 broadcast_select_fusion
  459.2 4.4 reshape.141
  463.6 6.3 multiply_reduce_fusion
  469.9 0.0 reduce-scatter.3.cloned.1.call-update
  470.0 0.3 reduce-scatter.5.cloned.1.call-start
  470.3 4.0 reshape.140
  474.2 5.3 reduce_sum.35
  479.6 0.0 reduce-scatter.5.cloned.1.call-update
  479.6 3.1 fusion.4
  482.7 1.7 fusion.2
  484.4 0.0 copy-done.7
  484.5 1.7 fusion.3
  486.2 85.3 %reduce-scatter.3.cloned.1.call-done = bf16[16,2560]{1,0:T(8,128)(2,1)} async-done(((bf16[128,2560]{1,0:T(8,128)(2,1)}), bf16[16,2560]{1,0:T(8,128)(2,1)}) %reduce-scatter.3.cloned.1.call-update) | async-done | bytes 81936 | tf_op jit(solution)/shard_map/reduce_scatter | solution.py:130
  571.5 92.1 %reduce-scatter.5.cloned.1.call-done = bf16[16,2560]{1,0:T(8,128)(2,1)} async-done(((bf16[128,2560]{1,0:T(8,128)(2,1)}), bf16[16,2560]{1,0:T(8,128)(2,1)}) %reduce-scatter.5.cloned.1.call-update) | async-done | bytes 81936 | tf_op jit(solution)/shard_map/reduce_scatter | solution.py:133
  (31 shorter events, 0.2 us)
Async XLA Ops:
  7.2 279.1 %copy-start = (bf16[1,128,2560]{2,1,0:T(8,128)(2,1)S(1)}, bf16[1,128,2560]{2,1,0:T(8,128)(2,1)}, u32[]{:S(2)}) copy-start(bf16[1,128,2560]{2,1,0:T(8,128)(2,1)} %param.15) | copy-start | bytes 1966084
  7.2 49.0 %copy-start.12 = (bf16[16,2]{0,1:T(2,128)(2,1)S(1)}, bf16[16,2]{0,1:T(2,128)(2,1)}, u32[]{:S(2)}) copy-start(bf16[16,2]{0,1:T(2,128)(2,1)} %param.12) | copy-start | bytes 196
  7.2 72.4 %copy-start.11 = (bf16[16,2560]{1,0:T(8,128)(2,1)S(1)}, bf16[16,2560]{1,0:T(8,128)(2,1)}, u32[]{:S(2)}) copy-start(bf16[16,2560]{1,0:T(8,128)(2,1)} %param.9) | copy-start | bytes 245764
  9.0 114.2 %all-to-all-start.2 = ((bf16[8,16,2560]{2,1,0:T(8,128)(2,1)}), bf16[8,16,2560]{2,1,0:T(8,128)(2,1)S(1)}, u32[]{:S(2)}, u32[]{:S(2)}) async-start(bf16[8,16,2560]{2,1,0:T(8,128)(2,1)} %stack.2), calls=%async_computation.3 | async-start | bytes 1310720 | tf_op jit(solution)/shard_map/all_to_all | solution.py:65
  79.0 0.6 copy-start.4
  211.7 74.6 %all-to-all-start.3 = ((bf16[64,8,2560]{2,1,0:T(8,128)(2,1)}), bf16[64,8,2560]{2,1,0:T(8,128)(2,1)}, u32[]{:S(2)}, u32[]{:S(2)}) async-start(bf16[64,8,2560]{2,1,0:T(8,128)(2,1)} %get-tuple-element.13), calls=%async_computation.4 | async-start | bytes 5242880 | tf_op jit(solution)/shard_map/all_to_all | solution.py:93
  224.5 2.0 copy-start.2
  286.3 3.3 copy-start.3
  289.6 0.9 copy-start.8
  289.6 0.9 copy-start.6
  289.6 1.2 copy-start.1
  293.1 16.5 %copy-start.10 = (bf16[512,128]{1,0:T(8,128)(2,1)S(1)}, bf16[512,128]{1,0:T(8,128)(2,1)}, u32[]{:S(2)}) copy-start(bf16[512,128]{1,0:T(8,128)(2,1)} %get-tuple-element.12) | copy-start | bytes 393220
  293.1 78.3 %all-to-all-start.4 = ((bf16[64,8,2560]{2,1,0:T(8,128)(2,1)}), bf16[64,8,2560]{2,1,0:T(8,128)(2,1)}, u32[]{:S(2)}, u32[]{:S(2)}) async-start(bf16[64,8,2560]{2,1,0:T(8,128)(2,1)} %fusion), calls=%async_computation.5 | async-start | bytes 5242880 | tf_op jit(solution)/shard_map/all_to_all | solution.py:116
  371.4 77.9 %all-to-all-start.1 = ((bf16[64,8,2560]{2,1,0:T(8,128)(2,1)}), bf16[64,8,2560]{2,1,0:T(8,128)(2,1)}, u32[]{:S(2)}, u32[]{:S(2)}) async-start(bf16[64,8,2560]{2,1,0:T(8,128)(2,1)} %fusion.1), calls=%async_computation.1 | async-start | bytes 5242880 | tf_op jit(solution)/shard_map/all_to_all | solution.py:109
  387.6 183.8 %reduce-scatter.3.cloned.1.call-start = ((), (), s32[]{:S(2)}) async-start(), calls=%async_computation.7 | async-start | bytes 737280 | tf_op jit(solution)/shard_map/reduce_scatter | solution.py:130
  459.2 4.4 copy-start.5
  470.0 193.6 %reduce-scatter.5.cloned.1.call-start = ((), (), s32[]{:S(2)}) async-start(), calls=%async_computation.8 | async-start | bytes 737280 | tf_op jit(solution)/shard_map/reduce_scatter | solution.py:133
  474.2 8.5 %copy-start.9 = (bf16[512,128]{1,0:T(8,128)(2,1)S(1)}, bf16[512,128]{1,0:T(8,128)(2,1)}, u32[]{:S(2)}) copy-start(bf16[512,128]{1,0:T(8,128)(2,1)} %copy-done.8) | copy-start | bytes 393220
  482.7 1.7 copy-start.7
Sparse Core Ops, SparseCore 0:
  470.1 101.3 reduce-scatter.2
  576.5 86.9 reduce-scatter.4
